TPU v7x, 256 devices: a whole 4x4x8 slice. The times are simulated.
256 devices in a mesh: seg: 128 (over y, x_hi, z, core), fsdp: 2 (over x_lo).
Axes of the slice: x: 4 (x_hi: 2, x_lo: 2; x = x_hi * 2 + x_lo), y: 4, z: 8, core: 2. Of those that a mesh axis runs over, the one named last changes fastest.
Arguments:
- hidden_states: bfloat16 [98304, 2048], P(('seg', 'fsdp'))
- queries: bfloat16 [98304, 2048], P(('seg', 'fsdp'))
- w_key: bfloat16 [2048, 2048], P('fsdp')
- w_value: bfloat16 [2048, 2048], P('fsdp'), may hold values from -0.125 to 0.125
Outputs:
- attended: bfloat16 [98304, 2048], P(('seg', 'fsdp'))
All inputs are finite; a program needn't handle non-finite values.
Results may differ from a plain program's by a relative error of at most 0.0076.
Values may be sent and summed in bfloat16 or wider, within the bound.
No kernel may reach another device: no remote copies, remote signals or barrier semaphores. Data moves between devices by JAX's collectives and lax.ppermute only.
A program may use at most 128 MiB of HBM per device.

v0:
```python
import jax
import jax.numpy as jnp
from jax import lax
from jax.sharding import PartitionSpec as P

HD = 128
MEM = 2


def from_behind(value, axis, steps):
    count = lax.axis_size(axis)
    leading, last = (max(0, -steps), min(count, count - steps))
    return lax.ppermute(value, axis, [(source, source + steps) for source in range(leading, last)])


def attend_group(query_rows, key_flat, value_flat, allowed, group_number):
    span = 4 * HD
    count = query_rows.shape[0]
    query_part = lax.dynamic_slice_in_dim(query_rows, group_number * span, span, 1).reshape(
        count, 4, HD
    )
    key_part = lax.dynamic_slice_in_dim(key_flat, group_number * span, span, 1).reshape(
        key_flat.shape[0], 4, HD
    )
    value_part = lax.dynamic_slice_in_dim(value_flat, group_number * span, span, 1).reshape(
        value_flat.shape[0], 4, HD
    )
    scores = jnp.einsum(
        "qhd,khd->hqk", query_part, key_part, preferred_element_type=jnp.float32
    ) * HD ** (-0.5)
    scores = jnp.where(allowed[None], scores, jnp.float32(-1e30))
    top_score = jnp.max(scores, axis=-1, keepdims=True)
    expo = jnp.where(allowed[None], jnp.exp(scores - top_score), jnp.float32(0.0))
    total = jnp.sum(expo, axis=-1)
    weights = expo.astype(jnp.bfloat16)
    mixed = jnp.einsum("hqk,khd->qhd", weights, value_part, preferred_element_type=jnp.float32)
    mixed = mixed / jnp.transpose(total)[:, :, None]
    return mixed.reshape(count, span).astype(jnp.bfloat16)


def body(hidden_states, queries, w_key, w_value):
    tok_rows = hidden_states.shape[0]
    width = w_key.shape[1]
    key_sum = jnp.dot(
        hidden_states,
        lax.all_gather(w_key, "fsdp", axis=0, tiled=True),
        preferred_element_type=jnp.float32,
    )
    value_sum = jnp.dot(
        hidden_states,
        lax.all_gather(w_value, "fsdp", axis=0, tiled=True),
        preferred_element_type=jnp.float32,
    )
    own_pair = jnp.stack([key_sum.astype(jnp.bfloat16), value_sum.astype(jnp.bfloat16)])
    own_unit = lax.all_gather(own_pair, "fsdp", axis=1, tiled=True)
    earlier = []
    for distance in range(1, MEM + 1):
        arrived = from_behind(own_unit, "seg", distance)
        earlier.insert(0, arrived)
    context = jnp.stack(earlier + [own_unit])
    seg_rows = context.shape[2]
    key_flat = context[:, 0].reshape((MEM + 1) * seg_rows, width)
    value_flat = context[:, 1].reshape((MEM + 1) * seg_rows, width)
    seg_number = lax.axis_index("seg")
    half_number = lax.axis_index("fsdp")
    query_pos = half_number * tok_rows + jnp.arange(tok_rows, dtype=jnp.int32)
    key_pos = jnp.arange((MEM + 1) * seg_rows, dtype=jnp.int32)
    block_of = key_pos // seg_rows
    within = key_pos % seg_rows
    earlier_ok = (block_of < MEM) & (seg_number >= MEM - block_of)
    own_ok = (block_of == MEM)[None, :] & (within[None, :] <= query_pos[:, None])
    allowed = earlier_ok[None, :] | own_ok

    def one_group(group_number):
        return attend_group(queries, key_flat, value_flat, allowed, group_number)

    grouped = lax.map(one_group, jnp.arange(width // (4 * HD), dtype=jnp.int32))
    return jnp.transpose(grouped, (1, 0, 2)).reshape(tok_rows, width)


def solution(mesh):
    placed = (P(("seg", "fsdp"), None), P(("seg", "fsdp"), None), P("fsdp", None), P("fsdp", None))
    return jax.shard_map(
        body, mesh=mesh, in_specs=placed, out_specs=P(("seg", "fsdp"), None), check_vma=False
    )
```

profile of v0, /device:TPU:8, one launch (start us, length us, event | category | flops | bytes accessed | tf_op | source)
XLA Modules:
  0.0 693.0 jit_solution(751616169947207539)
XLA Ops:
  8.1 113.0 %all-gather.4.cloned.1.call-done = bf16[2048,2048]{1,0:T(8,128)(2,1)} async-done(((bf16[1024,2048]{1,0:T(8,128)(2,1)}), bf16[2048,2048]{1,0:T(8,128)(2,1)}) %all-gather.4.cloned.1.call-update) | async-done | bytes 8388624 | tf_op jit(solution)/shard_map/all_gather | solution.py:46
  121.1 6.8 fusion.22
  127.9 105.1 %all-gather.6.cloned.1.call-done = bf16[2048,2048]{1,0:T(8,128)(2,1)} async-done(((bf16[1024,2048]{1,0:T(8,128)(2,1)}), bf16[2048,2048]{1,0:T(8,128)(2,1)}) %all-gather.6.cloned.1.call-update) | async-done | bytes 8388624 | tf_op jit(solution)/shard_map/all_gather | solution.py:51
  233.0 6.8 fusion.23
  241.8 86.6 %all-gather.8.cloned.1.call-done = bf16[2,768,2048]{2,1,0:T(8,128)(2,1)} async-done(((bf16[2,384,2048]{2,1,0:T(8,128)(2,1)}), bf16[2,768,2048]{2,1,0:T(8,128)(2,1)}) %all-gather.8.cloned.1.call-update) | async-done | bytes 6291472 | tf_op jit(solution)/shard_map/all_gather | solution.py:55
  334.0 139.5 %collective-permute-done = bf16[2,768,2048]{2,1,0:T(8,128)(2,1)} collective-permute-done((bf16[2,768,2048]{2,1,0:T(8,128)(2,1)}, bf16[2,768,2048]{2,1,0:T(8,128)(2,1)}, u32[]{:S(2)}, u32[]{:S(2)}) %collective-permute-start) | collective-permute-done | bytes 6291488 | tf_op jit(solution)/shard_map/ppermute | solution.py:13
  473.4 66.1 %collective-permute-done.1 = bf16[2,768,2048]{2,1,0:T(8,128)(2,1)} collective-permute-done((bf16[2,768,2048]{2,1,0:T(8,128)(2,1)}, bf16[2,768,2048]{2,1,0:T(8,128)(2,1)}, u32[]{:S(2)}, u32[]{:S(2)}) %collective-permute-start.1) | collective-permute-done | bytes 6291488 | tf_op jit(solution)/shard_map/ppermute | solution.py:13
  539.6 9.6 %pad_maximum_fusion = bf16[3,2,768,2048]{3,2,1,0:T(8,128)(2,1)S(1)} fusion(bf16[1,2,768,2048]{3,2,1,0:T(8,128)(2,1)} %bitcast.62, bf16[1,2,768,2048]{3,2,1,0:T(8,128)(2,1)} %bitcast.3, bf16[1,2,768,2048]{3,2,1,0:T(8,128)(2,1)} %bitcast.2), kind=kLoop, calls=%fused_computation.21 | loop fusion | flops 18874368 | bytes 37748736 | tf_op jit(solution)/shard_map/stack | solution.py:60
  549.2 6.8 fusion.33
  555.9 127.8 %while.11 = (s32[]{:T(128)}, bf16[4,384,512]{1,2,0:T(8,128)(2,1)}, s32[4]{0:T(128)S(1)}, bf16[2304,2048]{1,0:T(8,128)(2,1)}, bf16[384,2048]{1,0:T(8,128)(2,1)}, ...) while((s32[]{:T(128)}, bf16[4,384,512]{1,2,0:T(8,128)(2,1)}, ...), condition=%wide.region_3.4_spmd.clone, body=%wide.region_0.3_spmd.clone.sunk | while | flops 1836222720 | bytes 42692296 | solution.py:77
  557.2 4.1 constant_dynamic-slice_fusion.5
  561.2 4.3 copy.24
  568.3 10.5 %fusion.54 = (f32[4,384]{1,0:T(4,128)S(1)}, bf16[4,384,2304]{2,1,0:T(8,128)(2,1)}) fusion(pred[384,2304]{1,0:T(8,128)(4,1)S(1)} %and_or_fusion.2, bf16[384,4,128]{0,2,1:T(8,128)(2,1)} %bitcast.60, bf16[2304,4,128]{0,2,1:T(8,128)(2,1)} %bitcast.56), kind=kOutput, calls=%fused_computation.42.clone.1 | convolution fusion | flops 927205632 | bytes 10721280 | tf_op jit(solution)/shard_map/while/body/eval_jaxpr/sub | solution.py:33
  581.3 5.7 fusion.55
  589.1 4.1 constant_dynamic-slice_fusion.5
  593.2 4.3 copy.24
  600.2 10.5 %fusion.54 = (f32[4,384]{1,0:T(4,128)S(1)}, bf16[4,384,2304]{2,1,0:T(8,128)(2,1)}) fusion(pred[384,2304]{1,0:T(8,128)(4,1)S(1)} %and_or_fusion.2, bf16[384,4,128]{0,2,1:T(8,128)(2,1)} %bitcast.60, bf16[2304,4,128]{0,2,1:T(8,128)(2,1)} %bitcast.56), kind=kOutput, calls=%fused_computation.42.clone.1 | convolution fusion | flops 927205632 | bytes 10721280 | tf_op jit(solution)/shard_map/while/body/eval_jaxpr/sub | solution.py:33
  613.3 5.7 fusion.55
  625.1 4.3 copy.24
  632.2 10.5 %fusion.54 = (f32[4,384]{1,0:T(4,128)S(1)}, bf16[4,384,2304]{2,1,0:T(8,128)(2,1)}) fusion(pred[384,2304]{1,0:T(8,128)(4,1)S(1)} %and_or_fusion.2, bf16[384,4,128]{0,2,1:T(8,128)(2,1)} %bitcast.60, bf16[2304,4,128]{0,2,1:T(8,128)(2,1)} %bitcast.56), kind=kOutput, calls=%fused_computation.42.clone.1 | convolution fusion | flops 927205632 | bytes 10721280 | tf_op jit(solution)/shard_map/while/body/eval_jaxpr/sub | solution.py:33
  645.2 5.8 fusion.55
  657.1 4.3 copy.24
  664.1 10.5 %fusion.54 = (f32[4,384]{1,0:T(4,128)S(1)}, bf16[4,384,2304]{2,1,0:T(8,128)(2,1)}) fusion(pred[384,2304]{1,0:T(8,128)(4,1)S(1)} %and_or_fusion.2, bf16[384,4,128]{0,2,1:T(8,128)(2,1)} %bitcast.60, bf16[2304,4,128]{0,2,1:T(8,128)(2,1)} %bitcast.56), kind=kOutput, calls=%fused_computation.42.clone.1 | convolution fusion | flops 927205632 | bytes 10721280 | tf_op jit(solution)/shard_map/while/body/eval_jaxpr/sub | solution.py:33
  677.2 5.7 fusion.55
  (45 shorter events, 46.4 us)
Async XLA Ops:
  6.5 114.6 %copy-start = (bf16[384,2048]{1,0:T(8,128)(2,1)S(1)}, bf16[384,2048]{1,0:T(8,128)(2,1)}, u32[]{:S(2)}) copy-start(bf16[384,2048]{1,0:T(8,128)(2,1)} %param.6) | copy-start | bytes 4718596
  6.5 114.6 %all-gather.4.cloned.1.call-start = ((), (), s32[]{:S(2)}) async-start(), calls=%async_computation | async-start | bytes 12582912 | tf_op jit(solution)/shard_map/all_gather | solution.py:46
  7.3 225.7 %all-gather.6.cloned.1.call-start = ((), (), s32[]{:S(2)}) async-start(), calls=%async_computation.1 | async-start | bytes 12582912 | tf_op jit(solution)/shard_map/all_gather | solution.py:51
  8.0 320.3 %all-gather.8.cloned.1.call-start = ((), (), s32[]{:S(2)}) async-start(), calls=%async_computation.2 | async-start | bytes 9437184 | tf_op jit(solution)/shard_map/all_gather | solution.py:55
  328.3 145.1 %collective-permute-start = (bf16[2,768,2048]{2,1,0:T(8,128)(2,1)}, bf16[2,768,2048]{2,1,0:T(8,128)(2,1)}, u32[]{:S(2)}, u32[]{:S(2)}) collective-permute-start(bf16[2,768,2048]{2,1,0:T(8,128)(2,1)} %all-gather.8.cloned.1.call-done), channel_id=1, source_target_pairs={{0,4},{2,6},{4,8},{6,10},{8,12},{10,14},{12,16},{14,18},{16,20},{1... | collective-permute-start | bytes 18874376 | tf_op jit(solution)/shard_map/ppermute | solution.py:13
  331.8 207.8 %collective-permute-start.1 = (bf16[2,768,2048]{2,1,0:T(8,128)(2,1)}, bf16[2,768,2048]{2,1,0:T(8,128)(2,1)}, u32[]{:S(2)}, u32[]{:S(2)}) collective-permute-start(bf16[2,768,2048]{2,1,0:T(8,128)(2,1)} %all-gather.8.cloned.1.call-done), channel_id=1, source_target_pairs={{0,2},{2,4},{4,6},{6,8},{8,10},{10,12},{12,14},{14,16},{16,18},{18... | collective-permute-start | bytes 18874376 | tf_op jit(solution)/shard_map/ppermute | solution.py:13
  683.7 2.7 copy-start.1
Sparse Core Ops, SparseCore 0:
  9.1 111.9 all-gather.3
  122.9 110.0 all-gather.5
  241.9 86.4 all-gather.7
where the time goes:
time: 694 us; the launch traced here: 693 us
  waiting for transfers between devices  512 us (74%)
  matrix products  78.6 us (11%)
  local copies, waits for them, and re-layouts  66.5 us (10%)
  other arithmetic  14.6 us (2%)
  between operations  13.2 us (2%)
    ppermute x2, waiting for transfers between devices, from_behind(): lax.ppermute(value, axis, [(source, source + steps) for source in range(l...  206 us
    all_gather x1, waiting for transfers between devices, body(): lax.all_gather(w_key, 'fsdp', axis=0, tiled=True)  113 us
    all_gather x1, waiting for transfers between devices, body(): lax.all_gather(w_value, 'fsdp', axis=0, tiled=True)  105 us
    all_gather x1, waiting for transfers between devices, body(): own_unit = lax.all_gather(own_pair, 'fsdp', axis=1, tiled=True)  86.6 us
    sub x4, matrix products, attend_group(): scores - top_score  42 us
    dynamic_slice x8, local copies, waits for them, and re-layouts, attend_group(): lax.dynamic_slice_in_dim(key_flat, group_number * span, span, 1)  33.7 us
    dot_general x4, matrix products, attend_group(): jnp.einsum('hqk,khd->qhd', weights, value_part, preferred_element_type=jn...  23 us
  transfers between devices with their start and end apart: 5, of which 5 were waited for; matrix products, arithmetic and copies ran while one was open for 1% of the time, Pallas kernels for 0%

commit v1 on v0

--- a/solution.py
+++ b/solution.py
@@ -48,7 +48,9 @@
     )
     value_sum = jnp.dot(
         hidden_states,
-        lax.all_gather(w_value, "fsdp", axis=0, tiled=True),
+        jnp.concatenate(
+            lax.all_to_all(jnp.stack([w_value] * lax.axis_size("fsdp")), "fsdp", 0, 0), axis=0
+        ),
         preferred_element_type=jnp.float32,
     )
     own_pair = jnp.stack([key_sum.astype(jnp.bfloat16), value_sum.astype(jnp.bfloat16)])

time: 694 us -> 665 us (0.958)
  waiting for transfers between devices: 512 us -> 299 us
  blocking collectives: 0 us -> 179 us
  other arithmetic: 14.6 us -> 22.1 us
    all_to_all x0 -> x1, blocking collectives: none -> 179 us  [body(): lax.all_to_all(jnp.stack([w_value] * lax.axis_size('fsdp')), 'fsdp', 0, 0)]
    all_gather x1, waiting for transfers between devices: 113 us -> 4.6 us  [body(): lax.all_gather(w_key, 'fsdp', axis=0, tiled=True)]
    all_gather x1 -> x0, waiting for transfers between devices: 105 us -> none  [body(): lax.all_gather(w_value, 'fsdp', axis=0, tiled=True)]
    another operation x0 -> x1, other arithmetic: none -> 7.46 us  [body(): jnp.stack([w_value] * lax.axis_size('fsdp'))]
  transfers between devices with their start and end apart: 5 -> 4, of which waited for: 5 -> 4; matrix products, arithmetic and copies ran while one was open for 1% -> 2% of each run, Pallas kernels for 0% -> 0%
where the time goes in v1:
time: 665 us; the launch traced here: 664 us
  waiting for transfers between devices  299 us (45%)
  blocking collectives  179 us (27%)
  matrix products  75.2 us (11%)
  local copies, waits for them, and re-layouts  66.6 us (10%)
  other arithmetic  22.1 us (3%)
  between operations  13.5 us (2%)
    ppermute x2, waiting for transfers between devices, from_behind(): lax.ppermute(value, axis, [(source, source + steps) for source in range(l...  206 us
    all_to_all x1, blocking collectives, body(): lax.all_to_all(jnp.stack([w_value] * lax.axis_size('fsdp')), 'fsdp', 0, 0)  179 us
    all_gather x1, waiting for transfers between devices, body(): own_unit = lax.all_gather(own_pair, 'fsdp', axis=1, tiled=True)  88.5 us
    sub x4, matrix products, attend_group(): scores - top_score  42 us
    dynamic_slice x8, local copies, waits for them, and re-layouts, attend_group(): lax.dynamic_slice_in_dim(key_flat, group_number * span, span, 1)  33.7 us
    dot_general x4, matrix products, attend_group(): jnp.einsum('hqk,khd->qhd', weights, value_part, preferred_element_type=jn...  23 us
  transfers between devices with their start and end apart: 4, of which 4 were waited for; matrix products, arithmetic and copies ran while one was open for 2% of the time, Pallas kernels for 0%

profile of v1, /device:TPU:8, one launch (start us, length us, event | category | flops | bytes accessed | tf_op | source)
XLA Modules:
  0.0 664.4 jit_solution(13451190703903012209)
XLA Ops:
  7.3 7.5 %pad_maximum_fusion.1 = bf16[2,1024,2048]{2,1,0:T(8,128)(2,1)} fusion(bf16[1,1024,2048]{2,1,0:T(8,128)(2,1)} %bitcast.68), kind=kLoop, calls=%fused_computation.22 | loop fusion | flops 4194304 | bytes 12582912 | tf_op jit(solution)/shard_map/stack | solution.py:52
  14.8 179.3 %all_to_all.5 = bf16[2,1024,2048]{2,1,0:T(8,128)(2,1)S(1)} all-to-all(bf16[2,1024,2048]{2,1,0:T(8,128)(2,1)} %pad_maximum_fusion.1), channel_id=1, replica_groups=mesh['seg'=128,'fsdp'=2] {'fsdp'}, dimensions={0} | all-to-all | bytes 16777216 | tf_op jit(solution)/shard_map/all_to_all | solution.py:52
  197.5 4.6 all-gather.3.cloned.1.call-done
  202.1 6.8 %fusion.22 = bf16[1,384,2048]{2,1,0:T(8,128)(2,1)S(1)} fusion(bf16[384,2048]{1,0:T(8,128)(2,1)S(1)} %copy-done, bf16[2048,2048]{1,0:T(8,128)(2,1)} %all-gather.3.cloned.1.call-done), kind=kOutput, calls=%fused_computation.26 | convolution fusion | flops 3222011904 | bytes 11534336 | tf_op jit(solution)/shard_map/dot_general | solution.py:44
  210.9 88.5 %all-gather.5.cloned.1.call-done = bf16[2,768,2048]{2,1,0:T(8,128)(2,1)} async-done(((bf16[2,384,2048]{2,1,0:T(8,128)(2,1)}), bf16[2,768,2048]{2,1,0:T(8,128)(2,1)}) %all-gather.5.cloned.1.call-update) | async-done | bytes 6291472 | tf_op jit(solution)/shard_map/all_gather | solution.py:57
  305.0 139.5 %collective-permute-done = bf16[2,768,2048]{2,1,0:T(8,128)(2,1)} collective-permute-done((bf16[2,768,2048]{2,1,0:T(8,128)(2,1)}, bf16[2,768,2048]{2,1,0:T(8,128)(2,1)}, u32[]{:S(2)}, u32[]{:S(2)}) %collective-permute-start) | collective-permute-done | bytes 6291488 | tf_op jit(solution)/shard_map/ppermute | solution.py:13
  444.5 66.1 %collective-permute-done.1 = bf16[2,768,2048]{2,1,0:T(8,128)(2,1)} collective-permute-done((bf16[2,768,2048]{2,1,0:T(8,128)(2,1)}, bf16[2,768,2048]{2,1,0:T(8,128)(2,1)}, u32[]{:S(2)}, u32[]{:S(2)}) %collective-permute-start.1) | collective-permute-done | bytes 6291488 | tf_op jit(solution)/shard_map/ppermute | solution.py:13
  510.6 9.6 %pad_maximum_fusion = bf16[3,2,768,2048]{3,2,1,0:T(8,128)(2,1)S(1)} fusion(bf16[1,2,768,2048]{3,2,1,0:T(8,128)(2,1)} %bitcast.67, bf16[1,2,768,2048]{3,2,1,0:T(8,128)(2,1)} %bitcast.6, bf16[1,2,768,2048]{3,2,1,0:T(8,128)(2,1)} %bitcast.5), kind=kLoop, calls=%fused_computation.21 | loop fusion | flops 18874368 | bytes 37748736 | tf_op jit(solution)/shard_map/stack | solution.py:62
  520.2 6.7 %fusion.33 = (bf16[3,1,768,2048]{3,2,1,0:T(8,128)(2,1)}, bf16[3,1,768,2048]{3,2,1,0:T(8,128)(2,1)}) fusion(bf16[3,2,768,2048]{3,2,1,0:T(8,128)(2,1)S(1)} %pad_maximum_fusion), kind=kLoop, calls=%fused_computation.44 | loop fusion | bytes 37748736 | tf_op jit(solution)/shard_map/slice | solution.py:64
  526.9 128.0 %while.11 = (s32[]{:T(128)}, bf16[4,384,512]{1,2,0:T(8,128)(2,1)}, s32[4]{0:T(128)S(1)}, bf16[2304,2048]{1,0:T(8,128)(2,1)}, bf16[384,2048]{1,0:T(8,128)(2,1)}, ...) while((s32[]{:T(128)}, bf16[4,384,512]{1,2,0:T(8,128)(2,1)}, ...), condition=%wide.region_3.4_spmd.clone, body=%wide.region_0.3_spmd.clone.sunk | while | flops 1836222720 | bytes 42692296 | solution.py:79
  528.2 4.1 constant_dynamic-slice_fusion.5
  532.3 4.3 copy.27
  539.3 10.5 %fusion.54 = (f32[4,384]{1,0:T(4,128)S(1)}, bf16[4,384,2304]{2,1,0:T(8,128)(2,1)}) fusion(pred[384,2304]{1,0:T(8,128)(4,1)S(1)} %and_or_fusion.2, bf16[384,4,128]{0,2,1:T(8,128)(2,1)} %bitcast.64, bf16[2304,4,128]{0,2,1:T(8,128)(2,1)} %bitcast.60), kind=kOutput, calls=%fused_computation.43.clone.1 | convolution fusion | flops 927205632 | bytes 10721280 | tf_op jit(solution)/shard_map/while/body/eval_jaxpr/sub | solution.py:33
  552.4 5.7 fusion.55
  560.2 4.1 constant_dynamic-slice_fusion.5
  564.3 4.3 copy.27
  571.3 10.5 %fusion.54 = (f32[4,384]{1,0:T(4,128)S(1)}, bf16[4,384,2304]{2,1,0:T(8,128)(2,1)}) fusion(pred[384,2304]{1,0:T(8,128)(4,1)S(1)} %and_or_fusion.2, bf16[384,4,128]{0,2,1:T(8,128)(2,1)} %bitcast.64, bf16[2304,4,128]{0,2,1:T(8,128)(2,1)} %bitcast.60), kind=kOutput, calls=%fused_computation.43.clone.1 | convolution fusion | flops 927205632 | bytes 10721280 | tf_op jit(solution)/shard_map/while/body/eval_jaxpr/sub | solution.py:33
  584.4 5.8 fusion.55
  596.2 4.3 copy.27
  603.3 10.5 %fusion.54 = (f32[4,384]{1,0:T(4,128)S(1)}, bf16[4,384,2304]{2,1,0:T(8,128)(2,1)}) fusion(pred[384,2304]{1,0:T(8,128)(4,1)S(1)} %and_or_fusion.2, bf16[384,4,128]{0,2,1:T(8,128)(2,1)} %bitcast.64, bf16[2304,4,128]{0,2,1:T(8,128)(2,1)} %bitcast.60), kind=kOutput, calls=%fused_computation.43.clone.1 | convolution fusion | flops 927205632 | bytes 10721280 | tf_op jit(solution)/shard_map/while/body/eval_jaxpr/sub | solution.py:33
  616.3 5.8 fusion.55
  628.2 4.3 copy.27
  635.3 10.5 %fusion.54 = (f32[4,384]{1,0:T(4,128)S(1)}, bf16[4,384,2304]{2,1,0:T(8,128)(2,1)}) fusion(pred[384,2304]{1,0:T(8,128)(4,1)S(1)} %and_or_fusion.2, bf16[384,4,128]{0,2,1:T(8,128)(2,1)} %bitcast.64, bf16[2304,4,128]{0,2,1:T(8,128)(2,1)} %bitcast.60), kind=kOutput, calls=%fused_computation.43.clone.1 | convolution fusion | flops 927205632 | bytes 10721280 | tf_op jit(solution)/shard_map/while/body/eval_jaxpr/sub | solution.py:33
  648.3 5.7 fusion.55
  (44 shorter events, 49.1 us)
Async XLA Ops:
  6.5 187.6 %copy-start = (bf16[384,2048]{1,0:T(8,128)(2,1)S(1)}, bf16[384,2048]{1,0:T(8,128)(2,1)}, u32[]{:S(2)}) copy-start(bf16[384,2048]{1,0:T(8,128)(2,1)} %param.6) | copy-start | bytes 4718596
  6.5 195.6 %all-gather.3.cloned.1.call-start = ((), (), s32[]{:S(2)}) async-start(), calls=%async_computation.1 | async-start | bytes 12582912 | tf_op jit(solution)/shard_map/all_gather | solution.py:46
  7.3 292.1 %all-gather.5.cloned.1.call-start = ((), (), s32[]{:S(2)}) async-start(), calls=%async_computation.2 | async-start | bytes 9437184 | tf_op jit(solution)/shard_map/all_gather | solution.py:57
  299.4 145.1 %collective-permute-start = (bf16[2,768,2048]{2,1,0:T(8,128)(2,1)}, bf16[2,768,2048]{2,1,0:T(8,128)(2,1)}, u32[]{:S(2)}, u32[]{:S(2)}) collective-permute-start(bf16[2,768,2048]{2,1,0:T(8,128)(2,1)} %all-gather.5.cloned.1.call-done), channel_id=1, source_target_pairs={{0,4},{2,6},{4,8},{6,10},{8,12},{10,14},{12,16},{14,18},{16,20},{1... | collective-permute-start | bytes 18874376 | tf_op jit(solution)/shard_map/ppermute | solution.py:13
  302.8 207.8 %collective-permute-start.1 = (bf16[2,768,2048]{2,1,0:T(8,128)(2,1)}, bf16[2,768,2048]{2,1,0:T(8,128)(2,1)}, u32[]{:S(2)}, u32[]{:S(2)}) collective-permute-start(bf16[2,768,2048]{2,1,0:T(8,128)(2,1)} %all-gather.5.cloned.1.call-done), channel_id=1, source_target_pairs={{0,2},{2,4},{4,6},{6,8},{8,10},{10,12},{12,14},{14,16},{16,18},{18... | collective-permute-start | bytes 18874376 | tf_op jit(solution)/shard_map/ppermute | solution.py:13
  654.9 2.7 copy-start.1
Sparse Core Ops, SparseCore 0:
  9.1 192.9 all-gather.2
  211.0 88.2 all-gather.4
